TPU v7x, 512 devices: a whole 4x8x8 slice. The times are simulated.
512 devices in a mesh: shard: 128 (over y, z, core), tensor: 4 (over x).
Axes of the slice: x: 4, y: 8, z: 8, core: 2. Of those that a mesh axis runs over, the one named last changes fastest.
Arguments:
- big_grad: bfloat16 [32, 1280, 768], P(None, 'shard', 'tensor')
- big_weight: bfloat16 [32, 1280, 768], P(None, 'shard', 'tensor'), may hold values from -0.017944336 to 0.017944336
- big_moment: float32 [128, 768, 1280], P('shard', 'tensor'), may hold values from -6 to 6
- small_grad: bfloat16 [32, 1280, 192], P(None, 'shard')
- small_weight: bfloat16 [32, 1280, 192], P(None, 'shard'), may hold values from -0.15625 to 0.15625
- small_moment: float32 [128, 192, 1280], P('shard'), may hold values from -6 to 6
- owners: int32 [2, 32], replicated, may hold values from 0 to 127, as said below
- vec_parts: float32 [128, 43008], P('shard'), may hold values from -0.6 to 0.6
- vec_param: float32 [43008], P('shard'), may hold values from 0.5 to 1.5
- vec_first: float32 [43008], P('shard'), may hold values from -0.6 to 0.6
- vec_second: float32 [43008], P('shard'), may hold values from 0.01 to 1
Outputs:
- big_weight_new: bfloat16 [32, 1280, 768], P(None, 'shard', 'tensor')
- big_moment_new: float32 [128, 768, 1280], P('shard', 'tensor')
- small_weight_new: bfloat16 [32, 1280, 192], P(None, 'shard')
- small_moment_new: float32 [128, 192, 1280], P('shard')
- vec_param_new: float32 [43008], P('shard')
- vec_first_new: float32 [43008], P('shard')
- vec_second_new: float32 [43008], P('shard')
Inputs may be any that keep to these rules, and one draw needn't show every extreme that they name: `owners`: no shard index appears twice in the whole list (over both rows); each aligned group of four shard indices holds exactly one owner of each row; the first and the last shard index own a matrix.
All inputs are finite; a program needn't handle non-finite values.
Results may differ from a plain program's by a relative error of at most 0.0068.
Values may be sent and summed in bfloat16 or wider, within the bound.
No kernel may reach another device: no remote copies, remote signals or barrier semaphores. Data moves between devices by JAX's collectives and lax.ppermute only.
A program may use at most 64 MiB of HBM per device.

v0:
```python
import math
import jax
import jax.numpy as jnp
from jax import lax
from jax.sharding import PartitionSpec as P

D = 1280
ITERS = 2
newton_linear = 3.4445
newton_cubic = -4.775
newton_quintic = 2.0315
momentum_rate = 0.95
muon_rate = 0.05
weight_decay = 0.1
norm_epsilon = 1e-07
adam_rate = 0.004
first_decay = 0.9
second_decay = 0.95
adam_epsilon = 1e-08
first_correct = 0.99997343860111
second_correct = 0.99407947077967


def owner_table(owner_list, count):
    devices = lax.broadcasted_iota(jnp.int32, (count, owner_list.shape[0]), 0)
    return (devices == owner_list[None, :]).astype(jnp.bfloat16)


def route_rows(owner_map, pieces):
    flattened = pieces.reshape(pieces.shape[0], -1)
    routed = jnp.dot(owner_map, flattened, preferred_element_type=jnp.float32)
    return routed.astype(jnp.bfloat16).reshape((owner_map.shape[0],) + pieces.shape[1:])


def collect(owner_map, arrived):
    flattened = arrived.reshape(arrived.shape[0], -1)
    picked = lax.dot_general(
        owner_map, flattened, (((0,), (0,)), ((), ())), preferred_element_type=jnp.float32
    )
    return picked.astype(jnp.bfloat16).reshape((owner_map.shape[1],) + arrived.shape[1:])


def advance(arrived, moment, is_owner):
    gradient = arrived.T.astype(jnp.float32)
    renewed = momentum_rate * moment + gradient
    retained = jnp.where(is_owner, renewed, moment)
    blended = jnp.where(is_owner, gradient + momentum_rate * renewed, 0.0).astype(jnp.bfloat16).T
    return (retained, blended)


def normalized(field):
    values = field.astype(jnp.float32)
    squares = jnp.sum(values * values)
    return (values / (jnp.sqrt(squares) + norm_epsilon)).astype(jnp.bfloat16)


def gram_block(left_part, right_part):
    product = lax.dot_general(
        left_part, right_part, (((0,), (0,)), ((), ())), preferred_element_type=jnp.float32
    )
    return product.astype(jnp.bfloat16)


def poly_block(gram_part, gram_full):
    square = jnp.dot(gram_part, gram_full, preferred_element_type=jnp.float32)
    return (newton_cubic * gram_part.astype(jnp.float32) + newton_quintic * square).astype(
        jnp.bfloat16
    )


def newton_step(column_part, full_iterate, polynomial):
    product = lax.dot_general(
        full_iterate, polynomial, (((1,), (1,)), ((), ())), preferred_element_type=jnp.float32
    )
    return (newton_linear * column_part.astype(jnp.float32) + product).astype(jnp.bfloat16)


def small_newton(field):
    iterate = normalized(field)
    for iteration in range(ITERS):
        gram_full = gram_block(iterate, iterate)
        iterate = newton_step(iterate, iterate, poly_block(gram_full, gram_full))
    return iterate


def apply_update(weight, update):
    scale = 0.2 * math.sqrt(D)
    values = weight.astype(jnp.float32)
    return (
        values - muon_rate * (scale * update.astype(jnp.float32) + weight_decay * values)
    ).astype(jnp.bfloat16)


def gather_columns(column_part):
    return lax.all_gather(column_part, "tensor", axis=1, tiled=True)


def gather_gram(gram_part):
    return lax.all_gather(gram_part, "tensor", axis=0, tiled=True)


def per_device(
    big_grad,
    big_weight,
    big_moment,
    small_grad,
    small_weight,
    small_moment,
    owners,
    vec_parts,
    vec_param,
    vec_first,
    vec_second,
):
    shards = lax.axis_size("shard")
    shard_place = lax.axis_index("shard")
    column = lax.axis_index("tensor")
    block_width = big_grad.shape[2]
    rows_dev = big_grad.shape[1]
    matrices = big_grad.shape[0]
    joint_map = owner_table(jnp.concatenate([owners[0], owners[1]]), shards)
    joint_pieces = jnp.concatenate([big_grad, small_grad], axis=0)
    arrived = lax.all_to_all(
        route_rows(joint_map, joint_pieces), "shard", split_axis=0, concat_axis=1, tiled=True
    )[0]
    big_owner = jnp.any(owners[0] == shard_place)
    small_owner = jnp.any(owners[1] == shard_place)
    big_retained, big_blended = advance(arrived, big_moment[0], big_owner)
    small_retained, small_blended = advance(arrived, small_moment[0], small_owner)
    small_result = small_newton(small_blended)
    full_iterate = normalized(gather_columns(big_blended))
    for iteration in range(ITERS - 1):
        gram_full = gram_block(full_iterate, full_iterate)
        full_iterate = newton_step(full_iterate, full_iterate, poly_block(gram_full, gram_full))
    gram_full = gram_block(full_iterate, full_iterate)
    gram_rows = lax.dynamic_slice_in_dim(gram_full, column * block_width, block_width, 0)
    owned_part = lax.dynamic_slice_in_dim(full_iterate, column * block_width, block_width, 1)
    big_result = newton_step(owned_part, full_iterate, poly_block(gram_rows, gram_full))
    own_result = jnp.where(big_owner, big_result, small_result)
    returned = lax.all_to_all(
        own_result.reshape(shards, rows_dev, block_width),
        "shard",
        split_axis=0,
        concat_axis=0,
        tiled=True,
    )
    picked = collect(joint_map, returned)
    big_weight_new = apply_update(big_weight, picked[:matrices])
    small_weight_new = apply_update(small_weight, picked[matrices:])
    vec_pieces = vec_parts[0].reshape(shards, -1)
    grad_share = jnp.sum(
        lax.all_to_all(vec_pieces, "shard", split_axis=0, concat_axis=0, tiled=True), axis=0
    )
    first_new = first_decay * vec_first + (1.0 - first_decay) * grad_share
    second_new = second_decay * vec_second + (1.0 - second_decay) * grad_share * grad_share
    param_new = vec_param - adam_rate * (first_new / first_correct) / (
        jnp.sqrt(second_new / second_correct) + adam_epsilon
    )
    return (
        big_weight_new,
        big_retained[None],
        small_weight_new,
        small_retained[None],
        param_new,
        first_new,
        second_new,
    )


def solution(mesh):
    return jax.shard_map(
        per_device,
        mesh=mesh,
        in_specs=(
            P(None, "shard", "tensor"),
            P(None, "shard", "tensor"),
            P("shard", "tensor", None),
            P(None, "shard", None),
            P(None, "shard", None),
            P("shard", None, None),
            P(),
            P("shard", None),
            P("shard"),
            P("shard"),
            P("shard"),
        ),
        out_specs=(
            P(None, "shard", "tensor"),
            P("shard", "tensor", None),
            P(None, "shard", None),
            P("shard", None, None),
            P("shard"),
            P("shard"),
            P("shard"),
        ),
        check_vma=False,
    )
```

profile of v0, /device:TPU:1, one launch (start us, length us, event | category | flops | bytes accessed | tf_op | source)
XLA Modules:
  0.0 153.9 jit_solution(12986507688042528019)
XLA Ops:
  7.2 0.8 slice_bitcast_fusion.1
  7.9 1.0 pad_maximum_fusion
  9.2 0.4 reshape.45
  10.2 1.3 copy.34
  11.5 1.6 %reshape.59 = bf16[128,2,960]{2,1,0:T(2,128)(2,1)} reshape(bf16[128,10,192]{2,1,0:T(8,128)(2,1)S(1)} %copy.34) | data formatting | bytes 983040
  13.1 18.4 %all-to-all-start = ((bf16[128,2,960]{2,1,0:T(2,128)(2,1)}), bf16[128,2,960]{2,1,0:T(2,128)(2,1)S(1)}, u32[]{:S(2)}, u32[]{:S(2)}) async-start(bf16[128,2,960]{2,1,0:T(2,128)(2,1)} %reshape.59), calls=%async_computation | async-start | bytes 1048576 | tf_op jit(solution)/shard_map/all_to_all | solution.py:123
  31.6 0.6 compare_reduce_fusion.1
  32.2 18.7 %all-to-all-done = bf16[128,2,960]{2,1,0:T(2,128)(2,1)S(1)} async-done(((bf16[128,2,960]{2,1,0:T(2,128)(2,1)}), bf16[128,2,960]{2,1,0:T(2,128)(2,1)S(1)}, u32[]{:S(2)}, u32[]{:S(2)}) %all-to-all-start) | async-done | bytes 491552 | tf_op jit(solution)/shard_map/all_to_all | solution.py:123
  50.9 0.8 reshape.60
  52.1 0.4 copy.35
  52.5 0.8 copy-done.1
  53.3 4.9 %fusion.17 = (f32[1,192,1280]{2,1,0:T(8,128)}, bf16[1280,192]{0,1:T(8,128)(2,1)}, f32[1,192,1280]{2,1,0:T(8,128)}, f32[]{:T(128)}, bf16[192,1280]{1,0:T(8,128)(2,1)S(1)}) fusion(f32[1,192,1280]{2,1,0:T(8,128)S(1)} %copy-done.1, f32[1280,192]{0,1:T(8,128)S(1)} %copy.35, pred[]{:T(512)} %get-tuple-element.21, f32[1,192,1280]{2,1,0:T(8,128)} %param.16, ...), kind=kLoop, calls=%fused_computation.39 | loop fusion | flops 4177919 | bytes 5898246 | tf_op jit(solution)/shard_map/broadcast_in_dim | solution.py:161
  58.2 0.5 broadcast.71
  58.7 1.0 reduce.5
  59.8 1.0 all_to_all.20
  60.8 7.3 %all-to-all-start.2 = ((f32[128,1,336]{2,1,0:T(1,128)}), f32[128,1,336]{2,1,0:T(1,128)S(1)}, u32[]{:S(2)}, u32[]{:S(2)}) async-start(f32[128,1,336]{2,1,0:T(1,128)} %all_to_all.20), calls=%async_computation.2 | async-start | bytes 393216 | tf_op jit(solution)/shard_map/all_to_all | solution.py:152
  69.1 0.4 fusion.3
  69.8 0.4 fusion.4
  70.3 16.5 %all-gather.2.cloned.1.call-done = bf16[1280,768]{0,1:T(8,128)(2,1)} async-done(((bf16[1280,192]{0,1:T(8,128)(2,1)}), bf16[1280,768]{0,1:T(8,128)(2,1)}) %all-gather.2.cloned.1.call-update) | async-done | bytes 1966096 | tf_op jit(solution)/shard_map/all_gather | solution.py:95
  86.8 3.3 %fusion = f32[]{:T(128)} fusion(bf16[1280,768]{0,1:T(8,128)(2,1)} %all-gather.2.cloned.1.call-done), kind=kLoop, calls=%fused_computation.2 | loop fusion | flops 2949119 | bytes 1966084 | tf_op jit(solution)/shard_map/reduce_sum | solution.py:53
  90.8 2.8 %convolution_convert_fusion.3 = bf16[768,768]{1,0:T(8,128)(2,1)} fusion(bf16[1280,768]{0,1:T(8,128)(2,1)S(1)} %copy-done, f32[]{:T(128)S(6)} %add.66), kind=kOutput, calls=%fused_computation.16 | convolution fusion | flops 1513488384 | bytes 3145732 | tf_op jit(solution)/shard_map/dot_general | solution.py:58
  93.6 6.3 %add_convert_fusion = bf16[1280,768]{0,1:T(8,128)(2,1)} fusion(bf16[768,768]{1,0:T(8,128)(2,1)} %convolution_convert_fusion.3, f32[]{:T(128)S(6)} %add.66, bf16[1280,768]{0,1:T(8,128)(2,1)S(1)} %copy-done), kind=kOutput, calls=%fused_computation.4 | convolution fusion | flops 2428698624 | bytes 5111812 | tf_op jit(solution)/shard_map/dot_general | solution.py:72
  99.9 3.8 %convolution_convert_fusion.2 = bf16[768,768]{1,0:T(8,128)(2,1)S(1)} fusion(bf16[1280,768]{0,1:T(8,128)(2,1)} %add_convert_fusion), kind=kOutput, calls=%fused_computation.15 | convolution fusion | flops 1510539264 | bytes 3145728 | tf_op jit(solution)/shard_map/dot_general | solution.py:58
  103.7 3.2 %fusion.5 = bf16[1280,192]{0,1:T(8,128)(2,1)S(1)} fusion(bf16[1280,192]{0,1:T(8,128)(2,1)S(1)} %fusion.4, bf16[1280,768]{0,1:T(8,128)(2,1)} %add_convert_fusion, bf16[768,768]{1,0:T(8,128)(2,1)S(1)} %convolution_convert_fusion.2, s32[]{:T(128)S(6)} %select_n.39, pred[]{:T(512)} %get-tuple-element.21), kind=kOutput, calls=%fused_computation.11 | convolution fusion | flops 605945856 | bytes 5212160 | tf_op jit(solution)/shard_map/dot_general | solution.py:72
  107.5 1.6 %reshape.61 = bf16[128,2,960]{2,1,0:T(2,128)(2,1)} reshape(bf16[128,10,192]{2,1,0:T(8,128)(2,1)S(1)} %reshape.47) | data formatting | bytes 983040
  109.1 14.5 %all-to-all-start.1 = ((bf16[128,2,960]{2,1,0:T(2,128)(2,1)}), bf16[128,2,960]{2,1,0:T(2,128)(2,1)S(1)}, u32[]{:S(2)}, u32[]{:S(2)}) async-start(bf16[128,2,960]{2,1,0:T(2,128)(2,1)} %reshape.61), calls=%async_computation.1 | async-start | bytes 1048576 | tf_op jit(solution)/shard_map/all_to_all | solution.py:140
  123.7 0.6 divide_subtract_fusion
  124.3 18.6 %all-to-all-done.1 = bf16[128,2,960]{2,1,0:T(2,128)(2,1)S(1)} async-done(((bf16[128,2,960]{2,1,0:T(2,128)(2,1)}), bf16[128,2,960]{2,1,0:T(2,128)(2,1)S(1)}, u32[]{:S(2)}, u32[]{:S(2)}) %all-to-all-start.1) | async-done | bytes 491552 | tf_op jit(solution)/shard_map/all_to_all | solution.py:140
  143.0 0.8 reshape.62
  143.7 0.7 copy.37
  145.2 0.7 copy.40
  146.3 0.7 copy.41
  (36 shorter events, 3.6 us)
Async XLA Ops:
  10.2 21.4 %copy-start.5 = (s32[2,32]{1,0:T(2,128)S(1)}, s32[2,32]{1,0:T(2,128)}, u32[]{:S(2)}) copy-start(s32[2,32]{1,0:T(2,128)} %param.17) | copy-start | bytes 772
  13.1 37.8 %all-to-all-start = ((bf16[128,2,960]{2,1,0:T(2,128)(2,1)}), bf16[128,2,960]{2,1,0:T(2,128)(2,1)S(1)}, u32[]{:S(2)}, u32[]{:S(2)}) async-start(bf16[128,2,960]{2,1,0:T(2,128)(2,1)} %reshape.59), calls=%async_computation | async-start | bytes 1048576 | tf_op jit(solution)/shard_map/all_to_all | solution.py:123
  31.5 55.3 %all-gather.2.cloned.1.call-start = ((), (), s32[]{:S(2)}) async-start(), calls=%async_computation.3 | async-start | bytes 2457600 | tf_op jit(solution)/shard_map/all_gather | solution.py:95
  52.1 1.2 copy-start.1
  53.3 5.4 %copy-start.2 = (f32[1,43008]{1,0:T(1,128)S(1)}, f32[1,43008]{1,0:T(1,128)}, u32[]{:S(2)}) copy-start(f32[1,43008]{1,0:T(1,128)} %param.18) | copy-start | bytes 516100
  60.8 48.3 %all-to-all-start.2 = ((f32[128,1,336]{2,1,0:T(1,128)}), f32[128,1,336]{2,1,0:T(1,128)S(1)}, u32[]{:S(2)}, u32[]{:S(2)}) async-start(f32[128,1,336]{2,1,0:T(1,128)} %all_to_all.20), calls=%async_computation.2 | async-start | bytes 393216 | tf_op jit(solution)/shard_map/all_to_all | solution.py:152
  86.8 4.0 %copy-start = (bf16[1280,768]{0,1:T(8,128)(2,1)S(1)}, bf16[1280,768]{0,1:T(8,128)(2,1)}, u32[]{:S(2)}) copy-start(bf16[1280,768]{0,1:T(8,128)(2,1)} %all-gather.2.cloned.1.call-done) | copy-start | bytes 5898244
  107.2 16.5 %copy-start.6 = (f32[336]{0:T(512)S(1)}, f32[336]{0:T(512)}, u32[]{:S(2)}) copy-start(f32[336]{0:T(512)} %param.19) | copy-start | bytes 4036
  107.2 16.5 %copy-start.7 = (f32[336]{0:T(512)S(1)}, f32[336]{0:T(512)}, u32[]{:S(2)}) copy-start(f32[336]{0:T(512)} %param.20) | copy-start | bytes 4036
  107.2 16.5 %copy-start.8 = (f32[336]{0:T(512)S(1)}, f32[336]{0:T(512)}, u32[]{:S(2)}) copy-start(f32[336]{0:T(512)} %param.21) | copy-start | bytes 4036
  109.1 33.9 %all-to-all-start.1 = ((bf16[128,2,960]{2,1,0:T(2,128)(2,1)}), bf16[128,2,960]{2,1,0:T(2,128)(2,1)S(1)}, u32[]{:S(2)}, u32[]{:S(2)}) async-start(bf16[128,2,960]{2,1,0:T(2,128)(2,1)} %reshape.61), calls=%async_computation.1 | async-start | bytes 1048576 | tf_op jit(solution)/shard_map/all_to_all | solution.py:140
  143.7 1.3 copy-start.3
  144.8 1.3 copy-start.4
Sparse Core Ops, SparseCore 0:
  58.3 28.4 all-gather.1
where the time goes:
time: 154 us
  waiting for transfers between devices  53.9 us (35%)
  starting transfers between devices  40.2 us (26%)
  matrix products  18.2 us (12%)
  between operations  15.7 us (10%)
  local copies, waits for them, and re-layouts  13.7 us (9%)
  other arithmetic  12.2 us (8%)
    all_to_all x1, waiting for transfers between devices, per_device(): lax.all_to_all(route_rows(joint_map, joint_pieces), 'shard', split_axis=0...  18.7 us
    all_to_all x1, waiting for transfers between devices, per_device(): lax.all_to_all(own_result.reshape(shards, rows_dev, block_width), 'shard'...  18.6 us
    all_to_all x1, starting transfers between devices, per_device(): lax.all_to_all(route_rows(joint_map, joint_pieces), 'shard', split_axis=0...  18.4 us
    all_gather x1, waiting for transfers between devices, gather_columns(): return lax.all_gather(column_part, 'tensor', axis=1, tiled=True)  16.5 us
    all_to_all x1, starting transfers between devices, per_device(): lax.all_to_all(own_result.reshape(shards, rows_dev, block_width), 'shard'...  14.5 us
    dot_general x4, matrix products, newton_step(): lax.dot_general(full_iterate, polynomial, (((1,), (1,)), ((), ())), prefe...  10.4 us
    unnamed x25, local copies, waits for them, and re-layouts  7.42 us
    all_to_all x1, starting transfers between devices, per_device(): lax.all_to_all(vec_pieces, 'shard', split_axis=0, concat_axis=0, tiled=True)  7.25 us
  transfers between devices with their start and end apart: 4, of which 3 were waited for; matrix products, arithmetic and copies ran while one was open for 17% of the time, Pallas kernels for 0%

commit v1 on v0

--- a/solution.py
+++ b/solution.py
@@ -19,6 +19,13 @@
 adam_epsilon = 1e-08
 first_correct = 0.99997343860111
 second_correct = 0.99407947077967
+
+
+def show_forms(u_in):
+    block_now = lax.axis_size("shard")
+    built = jnp.split(u_in, block_now, axis=0)
+    next_value = lax.all_to_all(jnp.stack(built), axis_name="shard", split_axis=0, concat_axis=0)
+    return jnp.concatenate(next_value, axis=1)
 
 
 def owner_table(owner_list, count):
@@ -120,9 +127,7 @@
     matrices = big_grad.shape[0]
     joint_map = owner_table(jnp.concatenate([owners[0], owners[1]]), shards)
     joint_pieces = jnp.concatenate([big_grad, small_grad], axis=0)
-    arrived = lax.all_to_all(
-        route_rows(joint_map, joint_pieces), "shard", split_axis=0, concat_axis=1, tiled=True
-    )[0]
+    arrived = show_forms(route_rows(joint_map, joint_pieces))[0]
     big_owner = jnp.any(owners[0] == shard_place)
     small_owner = jnp.any(owners[1] == shard_place)
     big_retained, big_blended = advance(arrived, big_moment[0], big_owner)

time: 154 us -> 167 us (1.084)
  local copies, waits for them, and re-layouts: 13.7 us -> 25.6 us
    another operation x0 -> x129, local copies, waits for them, and re-layouts: none -> 11.2 us  [show_forms(): jnp.stack(built)]
    split x0 -> x7, local copies, waits for them, and re-layouts: none -> 2.72 us  [show_forms(): built = jnp.split(u_in, block_now, axis=0)]
    unnamed x25 -> x152, local copies, waits for them, and re-layouts: 7.42 us -> 7.82 us
  transfers between devices with their start and end apart: 4 -> 4, of which waited for: 3 -> 3; matrix products, arithmetic and copies ran while one was open for 17% -> 16% of each run, Pallas kernels for 0% -> 0%
where the time goes in v1:
time: 167 us
  waiting for transfers between devices  53.7 us (32%)
  starting transfers between devices  40.3 us (24%)
  local copies, waits for them, and re-layouts  25.6 us (15%)
  matrix products  18.2 us (11%)
  between operations  16.8 us (10%)
  other arithmetic  12.2 us (7%)
    all_to_all x1, waiting for transfers between devices, per_device(): lax.all_to_all(own_result.reshape(shards, rows_dev, block_width), 'shard'...  18.6 us
    all_to_all x1, waiting for transfers between devices, show_forms(): lax.all_to_all(jnp.stack(built), axis_name='shard', split_axis=0, concat_...  18.6 us
    all_to_all x1, starting transfers between devices, show_forms(): lax.all_to_all(jnp.stack(built), axis_name='shard', split_axis=0, concat_...  18.4 us
    all_gather x1, waiting for transfers between devices, gather_columns(): return lax.all_gather(column_part, 'tensor', axis=1, tiled=True)  16.6 us
    all_to_all x1, starting transfers between devices, per_device(): lax.all_to_all(own_result.reshape(shards, rows_dev, block_width), 'shard'...  14.5 us
    another operation x129, local copies, waits for them, and re-layouts, show_forms(): jnp.stack(built)  11.2 us
    dot_general x4, matrix products, newton_step(): lax.dot_general(full_iterate, polynomial, (((1,), (1,)), ((), ())), prefe...  10.4 us
    unnamed x152, local copies, waits for them, and re-layouts  7.82 us
  transfers between devices with their start and end apart: 4, of which 3 were waited for; matrix products, arithmetic and copies ran while one was open for 16% of the time, Pallas kernels for 0%

profile of v1, /device:TPU:1, one launch (start us, length us, event | category | flops | bytes accessed | tf_op | source)
XLA Modules:
  0.0 166.8 jit_solution(8958094974873119535)
XLA Ops:
  7.2 1.0 pad_maximum_fusion
  9.5 0.4 slice_reduce_fusion.95
  9.9 0.4 slice_reduce_fusion.76
  10.7 0.4 slice_reduce_fusion.38
  11.1 0.4 slice_reduce_fusion.19
  24.6 1.6 reshape.436
  26.1 18.4 %all-to-all-start = ((bf16[128,2,960]{2,1,0:T(2,128)(2,1)}), bf16[128,2,960]{2,1,0:T(2,128)(2,1)S(1)}, u32[]{:S(2)}, u32[]{:S(2)}) async-start(bf16[128,2,960]{2,1,0:T(2,128)(2,1)} %reshape.436), calls=%async_computation | async-start | bytes 1048576 | tf_op jit(solution)/shard_map/all_to_all | solution.py:27
  44.8 0.6 compare_reduce_fusion.1
  45.4 18.6 %all-to-all-done = bf16[128,2,960]{2,1,0:T(2,128)(2,1)S(1)} async-done(((bf16[128,2,960]{2,1,0:T(2,128)(2,1)}), bf16[128,2,960]{2,1,0:T(2,128)(2,1)S(1)}, u32[]{:S(2)}, u32[]{:S(2)}) %all-to-all-start) | async-done | bytes 491552 | tf_op jit(solution)/shard_map/all_to_all | solution.py:27
  64.0 0.8 reshape.437
  65.5 0.8 copy-done.1
  66.3 4.9 %fusion.17 = (f32[1,192,1280]{2,1,0:T(8,128)}, bf16[1280,192]{0,1:T(8,128)(2,1)}, f32[1,192,1280]{2,1,0:T(8,128)}, f32[]{:T(128)}, bf16[192,1280]{1,0:T(8,128)(2,1)S(1)}) fusion(f32[1,192,1280]{2,1,0:T(8,128)S(1)} %copy-done.1, f32[1280,192]{0,1:T(8,128)S(1)} %copy.297, pred[]{:T(512)} %get-tuple-element.156, f32[1,192,1280]{2,1,0:T(8,128)} %param.16, ...), kind=kLoop, calls=%fused_computation.39 | loop fusion | flops 4177919 | bytes 5898246 | tf_op jit(solution)/shard_map/broadcast_in_dim | solution.py:166
  71.2 0.5 broadcast.199
  71.7 1.0 reduce.261
  72.8 1.0 all_to_all.16
  73.8 7.2 %all-to-all-start.2 = ((f32[128,1,336]{2,1,0:T(1,128)}), f32[128,1,336]{2,1,0:T(1,128)S(1)}, u32[]{:S(2)}, u32[]{:S(2)}) async-start(f32[128,1,336]{2,1,0:T(1,128)} %all_to_all.16), calls=%async_computation.2 | async-start | bytes 393216 | tf_op jit(solution)/shard_map/all_to_all | solution.py:157
  82.1 0.4 fusion.3
  82.8 0.4 fusion.4
  83.3 16.6 %all-gather.2.cloned.1.call-done = bf16[1280,768]{0,1:T(8,128)(2,1)} async-done(((bf16[1280,192]{0,1:T(8,128)(2,1)}), bf16[1280,768]{0,1:T(8,128)(2,1)}) %all-gather.2.cloned.1.call-update) | async-done | bytes 1966096 | tf_op jit(solution)/shard_map/all_gather | solution.py:102
  99.8 3.3 %fusion = f32[]{:T(128)} fusion(bf16[1280,768]{0,1:T(8,128)(2,1)} %all-gather.2.cloned.1.call-done), kind=kLoop, calls=%fused_computation.2 | loop fusion | flops 2949119 | bytes 1966084 | tf_op jit(solution)/shard_map/reduce_sum | solution.py:60
  103.8 2.8 %convolution_convert_fusion.3 = bf16[768,768]{1,0:T(8,128)(2,1)} fusion(bf16[1280,768]{0,1:T(8,128)(2,1)S(1)} %copy-done, f32[]{:T(128)S(6)} %add.66), kind=kOutput, calls=%fused_computation.16 | convolution fusion | flops 1513488384 | bytes 3145732 | tf_op jit(solution)/shard_map/dot_general | solution.py:65
  106.6 6.3 %add_convert_fusion = bf16[1280,768]{0,1:T(8,128)(2,1)} fusion(bf16[768,768]{1,0:T(8,128)(2,1)} %convolution_convert_fusion.3, f32[]{:T(128)S(6)} %add.66, bf16[1280,768]{0,1:T(8,128)(2,1)S(1)} %copy-done), kind=kOutput, calls=%fused_computation.4 | convolution fusion | flops 2428698624 | bytes 5111812 | tf_op jit(solution)/shard_map/dot_general | solution.py:79
  112.9 3.8 %convolution_convert_fusion.2 = bf16[768,768]{1,0:T(8,128)(2,1)S(1)} fusion(bf16[1280,768]{0,1:T(8,128)(2,1)} %add_convert_fusion), kind=kOutput, calls=%fused_computation.15 | convolution fusion | flops 1510539264 | bytes 3145728 | tf_op jit(solution)/shard_map/dot_general | solution.py:65
  116.7 3.2 %fusion.5 = bf16[1280,192]{0,1:T(8,128)(2,1)S(1)} fusion(bf16[1280,192]{0,1:T(8,128)(2,1)S(1)} %fusion.4, bf16[1280,768]{0,1:T(8,128)(2,1)} %add_convert_fusion, bf16[768,768]{1,0:T(8,128)(2,1)S(1)} %convolution_convert_fusion.2, s32[]{:T(128)S(6)} %select_n.39, pred[]{:T(512)} %get-tuple-element.156), kind=kOutput, calls=%fused_computation.11 | convolution fusion | flops 605945856 | bytes 5212160 | tf_op jit(solution)/shard_map/dot_general | solution.py:79
  120.5 1.6 reshape.438
  122.1 14.5 %all-to-all-start.1 = ((bf16[128,2,960]{2,1,0:T(2,128)(2,1)}), bf16[128,2,960]{2,1,0:T(2,128)(2,1)S(1)}, u32[]{:S(2)}, u32[]{:S(2)}) async-start(bf16[128,2,960]{2,1,0:T(2,128)(2,1)} %reshape.438), calls=%async_computation.1 | async-start | bytes 1048576 | tf_op jit(solution)/shard_map/all_to_all | solution.py:145
  136.7 0.6 divide_subtract_fusion
  137.3 18.6 %all-to-all-done.1 = bf16[128,2,960]{2,1,0:T(2,128)(2,1)S(1)} async-done(((bf16[128,2,960]{2,1,0:T(2,128)(2,1)}), bf16[128,2,960]{2,1,0:T(2,128)(2,1)S(1)}, u32[]{:S(2)}, u32[]{:S(2)}) %all-to-all-start.1) | async-done | bytes 491552 | tf_op jit(solution)/shard_map/all_to_all | solution.py:145
  155.9 0.8 reshape.439
  156.7 0.7 copy.299
  158.2 0.7 copy.302
  159.3 0.7 copy.303
  (297 shorter events, 17.0 us)
Async XLA Ops:
  7.2 1.6 copy-start.5
  26.1 37.8 %all-to-all-start = ((bf16[128,2,960]{2,1,0:T(2,128)(2,1)}), bf16[128,2,960]{2,1,0:T(2,128)(2,1)S(1)}, u32[]{:S(2)}, u32[]{:S(2)}) async-start(bf16[128,2,960]{2,1,0:T(2,128)(2,1)} %reshape.436), calls=%async_computation | async-start | bytes 1048576 | tf_op jit(solution)/shard_map/all_to_all | solution.py:27
  44.5 55.3 %all-gather.2.cloned.1.call-start = ((), (), s32[]{:S(2)}) async-start(), calls=%async_computation.3 | async-start | bytes 2457600 | tf_op jit(solution)/shard_map/all_gather | solution.py:102
  65.1 1.2 copy-start.1
  66.3 5.4 %copy-start.2 = (f32[1,43008]{1,0:T(1,128)S(1)}, f32[1,43008]{1,0:T(1,128)}, u32[]{:S(2)}) copy-start(f32[1,43008]{1,0:T(1,128)} %param.18) | copy-start | bytes 516100
  73.8 48.3 %all-to-all-start.2 = ((f32[128,1,336]{2,1,0:T(1,128)}), f32[128,1,336]{2,1,0:T(1,128)S(1)}, u32[]{:S(2)}, u32[]{:S(2)}) async-start(f32[128,1,336]{2,1,0:T(1,128)} %all_to_all.16), calls=%async_computation.2 | async-start | bytes 393216 | tf_op jit(solution)/shard_map/all_to_all | solution.py:157
  99.8 4.0 %copy-start = (bf16[1280,768]{0,1:T(8,128)(2,1)S(1)}, bf16[1280,768]{0,1:T(8,128)(2,1)}, u32[]{:S(2)}) copy-start(bf16[1280,768]{0,1:T(8,128)(2,1)} %all-gather.2.cloned.1.call-done) | copy-start | bytes 5898244
  120.2 16.5 %copy-start.6 = (f32[336]{0:T(512)S(1)}, f32[336]{0:T(512)}, u32[]{:S(2)}) copy-start(f32[336]{0:T(512)} %param.19) | copy-start | bytes 4036
  120.2 16.5 %copy-start.7 = (f32[336]{0:T(512)S(1)}, f32[336]{0:T(512)}, u32[]{:S(2)}) copy-start(f32[336]{0:T(512)} %param.20) | copy-start | bytes 4036
  120.2 16.5 %copy-start.8 = (f32[336]{0:T(512)S(1)}, f32[336]{0:T(512)}, u32[]{:S(2)}) copy-start(f32[336]{0:T(512)} %param.21) | copy-start | bytes 4036
  122.1 33.9 %all-to-all-start.1 = ((bf16[128,2,960]{2,1,0:T(2,128)(2,1)}), bf16[128,2,960]{2,1,0:T(2,128)(2,1)S(1)}, u32[]{:S(2)}, u32[]{:S(2)}) async-start(bf16[128,2,960]{2,1,0:T(2,128)(2,1)} %reshape.438), calls=%async_computation.1 | async-start | bytes 1048576 | tf_op jit(solution)/shard_map/all_to_all | solution.py:145
  156.7 1.3 copy-start.3
  157.8 1.3 copy-start.4
Sparse Core Ops, SparseCore 0:
  71.3 28.4 all-gather.1
